TPU v7x, 512 devices: a whole 4x8x8 slice. The times are simulated.
512 devices in a mesh: frame: 8 (over y), space: 32 (over z, x), dp: 2 (over core).
Axes of the slice: x: 4, y: 8, z: 8, core: 2. Of those that a mesh axis runs over, the one named last changes fastest.
Arguments:
- frames_in: bfloat16 [16, 4096, 768], P(('dp', 'frame'), 'space'), parts along dimension 0, may hold values from -6 to 6
- cotangent: bfloat16 [16, 4096, 768], P(('dp', 'frame'), 'space'), parts along dimension 0, may hold values from -6 to 6
- w_qkv_space: bfloat16 [768, 2304], P('space'), may hold values from -0.21875 to 0.21875
- w_out_space: bfloat16 [768, 768], P('space'), may hold values from -0.875 to 0.875
- w_qkv_time: bfloat16 [768, 2304], P('space'), may hold values from -0.21875 to 0.21875
- w_out_time: bfloat16 [768, 768], P('space'), may hold values from -0.21875 to 0.21875
- neighbours: int32 [32, 4], replicated, may hold values from 0 to 31, as said below
Outputs:
- frames_out: bfloat16 [16, 4096, 768], P(('dp', 'frame'), 'space'), parts along dimension 0
- grad_frames: bfloat16 [16, 4096, 768], P(('dp', 'frame'), 'space'), parts along dimension 0
There are 2 independent parts, one for each index of `dp`. A program takes and returns all parts, laid end to end along the dimension named above; an argument that names none is the same for every part. Nothing has to cross between parts.
Inputs may be any that keep to these rules, and one draw needn't show every extreme that they name: `neighbours`: row b lists block b first; every entry c satisfies |c - b| <= 1; entries may repeat, and a repeated entry counts once.
All inputs are finite; a program needn't handle non-finite values.
Results may differ from a plain program's by a relative error of at most 0.023.
Values may be sent and summed in bfloat16 or wider, within the bound.
No kernel may reach another device: no remote copies, remote signals or barrier semaphores. Data moves between devices by JAX's collectives and lax.ppermute only.
A program may use at most 64 MiB of HBM per device.

v0:
```python
import jax
import jax.numpy as jnp
from jax import lax
from jax.sharding import PartitionSpec as P

HEADS = 12
HD = 64
BLOCK = 128
EPS = 1e-06


def padded(cells, sides, width):
    for axis, dim in sides:
        count = lax.axis_size(axis)
        ends = count - 1
        head = lax.slice_in_dim(cells, 0, width, axis=dim)
        tail = lax.slice_in_dim(cells, cells.shape[dim] - width, cells.shape[dim], axis=dim)
        cells = jnp.concatenate(
            [
                lax.ppermute(tail, axis, [(i, (i + 1) % count) for i in range(ends)]),
                cells,
                lax.ppermute(head, axis, [((i + 1) % count, i) for i in range(ends)]),
            ],
            axis=dim,
        )
    return cells


def rms_norm(row_data):
    values = row_data.astype(jnp.float32)
    factor = lax.rsqrt(jnp.mean(values * values, axis=-1, keepdims=True) + EPS)
    return (values * factor).astype(jnp.bfloat16)


def rms_back(row_data, upstream):
    values = row_data.astype(jnp.float32)
    factor = lax.rsqrt(jnp.mean(values * values, axis=-1, keepdims=True) + EPS)
    inner_mean = jnp.mean(values * upstream, axis=-1, keepdims=True)
    return factor * upstream - values * factor**3 * inner_mean


def block_mask(neighbour_rows, first_id):
    block_count = neighbour_rows.shape[0]
    candidate = first_id + jnp.arange(3 * block_count, dtype=jnp.int32)
    matches = jnp.any(neighbour_rows[:, :, None] == candidate[None, None, :], axis=1)
    return jnp.repeat(jnp.repeat(matches, BLOCK, axis=0), BLOCK, axis=1)


def space_attend(queries, key_rows, value_rows, allowed):
    score_scale = HD ** (-0.5)
    query_count = queries.shape[0]
    key_count = key_rows.shape[0]
    output_list = []
    total_list = []
    for head_pair in range(HEADS // 2):
        start_col = head_pair * 2 * HD
        stop_col = start_col + 2 * HD
        query_part = queries[:, start_col:stop_col].reshape(query_count, 2, HD)
        key_part = key_rows[:, start_col:stop_col].reshape(key_count, 2, HD)
        value_part = value_rows[:, start_col:stop_col].reshape(key_count, 2, HD)
        scores = (
            jnp.einsum("sgh,tgh->gst", query_part, key_part, preferred_element_type=jnp.float32)
            * score_scale
        )
        exponent = jnp.where(allowed[None], jnp.exp(scores), 0.0)
        totals = jnp.sum(exponent, axis=-1)
        probability = (exponent / totals[:, :, None]).astype(jnp.bfloat16)
        combined = jnp.einsum(
            "gst,tgh->sgh", probability, value_part, preferred_element_type=jnp.float32
        )
        output_list.append(combined.astype(jnp.bfloat16).reshape(query_count, 2 * HD))
        total_list.append(totals)
    return (jnp.concatenate(output_list, axis=1), jnp.concatenate(total_list, axis=0))


def space_back(queries, key_rows, value_rows, allowed, totals, attended, grad_attended):
    score_scale = HD ** (-0.5)
    query_count = queries.shape[0]
    key_count = key_rows.shape[0]
    query_list = []
    key_list = []
    value_list = []
    for head_pair in range(HEADS // 2):
        start_col = head_pair * 2 * HD
        stop_col = start_col + 2 * HD
        query_part = queries[:, start_col:stop_col].reshape(query_count, 2, HD)
        key_part = key_rows[:, start_col:stop_col].reshape(key_count, 2, HD)
        value_part = value_rows[:, start_col:stop_col].reshape(key_count, 2, HD)
        out_part = attended[:, start_col:stop_col].reshape(query_count, 2, HD)
        grad_part = grad_attended[:, start_col:stop_col].reshape(query_count, 2, HD)
        scores = (
            jnp.einsum("sgh,tgh->gst", query_part, key_part, preferred_element_type=jnp.float32)
            * score_scale
        )
        exponent = jnp.where(allowed[None], jnp.exp(scores), 0.0)
        weight = exponent / totals[2 * head_pair : 2 * head_pair + 2, :, None]
        probability = weight.astype(jnp.bfloat16)
        prob_grad = jnp.einsum(
            "sgh,tgh->gst", grad_part, value_part, preferred_element_type=jnp.float32
        )
        row_delta = jnp.einsum(
            "sgh,sgh->gs", grad_part, out_part, preferred_element_type=jnp.float32
        )
        score_grad = (weight * (prob_grad - row_delta[:, :, None])).astype(jnp.bfloat16)
        query_grad = (
            jnp.einsum("gst,tgh->sgh", score_grad, key_part, preferred_element_type=jnp.float32)
            * score_scale
        )
        key_grad = (
            jnp.einsum("gst,sgh->tgh", score_grad, query_part, preferred_element_type=jnp.float32)
            * score_scale
        )
        value_grad = jnp.einsum(
            "gst,sgh->tgh", probability, grad_part, preferred_element_type=jnp.float32
        )
        query_list.append(query_grad.astype(jnp.bfloat16).reshape(query_count, 2 * HD))
        key_list.append(key_grad.reshape(key_count, 2 * HD))
        value_list.append(value_grad.reshape(key_count, 2 * HD))
    return (
        jnp.concatenate(query_list, axis=1),
        jnp.concatenate(key_list, axis=1),
        jnp.concatenate(value_list, axis=1),
    )


def time_attend(queries, key_rows, value_rows):
    frame_count, position_count, feature_count = queries.shape
    split_shape = (frame_count, position_count, HEADS, HD)
    score_scale = HD ** (-0.5)
    scores = (
        jnp.einsum(
            "fphd,gphd->phfg",
            queries.reshape(split_shape),
            key_rows.reshape(split_shape),
            preferred_element_type=jnp.float32,
        )
        * score_scale
    )
    causal = jnp.arange(frame_count)[:, None] >= jnp.arange(frame_count)[None, :]
    exponent = jnp.where(causal, jnp.exp(scores), 0.0)
    totals = jnp.sum(exponent, axis=-1)
    probability = (exponent / totals[..., None]).astype(jnp.bfloat16)
    combined = jnp.einsum(
        "phfg,gphd->fphd",
        probability,
        value_rows.reshape(split_shape),
        preferred_element_type=jnp.float32,
    )
    return (
        combined.astype(jnp.bfloat16).reshape(frame_count, position_count, feature_count),
        totals,
    )


def time_back(queries, key_rows, value_rows, attended, grad_attended, totals):
    frame_count, position_count, feature_count = queries.shape
    split_shape = (frame_count, position_count, HEADS, HD)
    score_scale = HD ** (-0.5)
    query_four = queries.reshape(split_shape)
    key_four = key_rows.reshape(split_shape)
    value_four = value_rows.reshape(split_shape)
    out_four = attended.reshape(split_shape)
    grad_four = grad_attended.reshape(split_shape)
    scores = (
        jnp.einsum("fphd,gphd->phfg", query_four, key_four, preferred_element_type=jnp.float32)
        * score_scale
    )
    causal = jnp.arange(frame_count)[:, None] >= jnp.arange(frame_count)[None, :]
    exponent = jnp.where(causal, jnp.exp(scores), 0.0)
    weight = exponent / totals[..., None]
    probability = weight.astype(jnp.bfloat16)
    prob_grad = jnp.einsum(
        "fphd,gphd->phfg", grad_four, value_four, preferred_element_type=jnp.float32
    )
    row_delta = jnp.einsum(
        "fphd,fphd->phf", grad_four, out_four, preferred_element_type=jnp.float32
    )
    score_grad = (weight * (prob_grad - row_delta[..., None])).astype(jnp.bfloat16)
    query_grad = (
        jnp.einsum("phfg,gphd->fphd", score_grad, key_four, preferred_element_type=jnp.float32)
        * score_scale
    )
    key_grad = (
        jnp.einsum("phfg,fphd->gphd", score_grad, query_four, preferred_element_type=jnp.float32)
        * score_scale
    )
    value_grad = jnp.einsum(
        "phfg,fphd->gphd", probability, grad_four, preferred_element_type=jnp.float32
    )
    pieces = [
        gradient.astype(jnp.bfloat16).reshape(frame_count, position_count, feature_count)
        for gradient in (query_grad, key_grad, value_grad)
    ]
    return jnp.concatenate(pieces, axis=-1)


def to_frames(local_rows):
    return lax.all_to_all(local_rows[None], "frame", split_axis=1, concat_axis=0, tiled=True)


def to_space(frame_rows):
    return lax.all_to_all(frame_rows, "frame", split_axis=0, concat_axis=1, tiled=True)[0]


def rim(first_part, second_part, width):
    return (padded(first_part, (("space", 0),), width), padded(second_part, (("space", 0),), width))


def local(frames_in, cotangent, w_qkv_space, w_out_space, w_qkv_time, w_out_time, neighbours):
    local_in = frames_in[0]
    grad_out = cotangent[0]
    shard, feature_count = local_in.shape
    weight_rows = jnp.concatenate([w_qkv_space, w_out_space, w_qkv_time, w_out_time], axis=1)
    all_weights = lax.all_gather(weight_rows, "space", axis=0, tiled=True)
    widths = [w_qkv_space.shape[1], w_out_space.shape[1], w_qkv_time.shape[1], w_out_time.shape[1]]
    bounds = [0]
    for width in widths:
        bounds.append(bounds[-1] + width)
    full_qkv_space, full_out_space, full_qkv_time, full_out_time = (
        all_weights[:, bounds[index] : bounds[index + 1]] for index in range(4)
    )
    block_count = shard // BLOCK
    space_index = lax.axis_index("space")
    lists_here = lax.dynamic_slice_in_dim(neighbours, space_index * block_count, block_count, 0)
    allowed = block_mask(lists_here, (space_index - 1) * block_count)
    normed_space = rms_norm(local_in)
    projected = jnp.dot(normed_space, full_qkv_space, preferred_element_type=jnp.float32).astype(
        jnp.bfloat16
    )
    queries = projected[:, :feature_count]
    key_window, value_window = rim(
        projected[:, feature_count : 2 * feature_count], projected[:, 2 * feature_count :], shard
    )
    attended, totals = space_attend(queries, key_window, value_window, allowed)
    update = jnp.dot(attended, full_out_space, preferred_element_type=jnp.float32)
    stream = (local_in.astype(jnp.float32) + update).astype(jnp.bfloat16)
    normed_time = rms_norm(stream)
    projected_time = jnp.dot(normed_time, full_qkv_time, preferred_element_type=jnp.float32).astype(
        jnp.bfloat16
    )
    time_rows = to_frames(projected_time)
    query_time = time_rows[..., :feature_count]
    key_time = time_rows[..., feature_count : 2 * feature_count]
    value_time = time_rows[..., 2 * feature_count :]
    attended_time, totals_time = time_attend(query_time, key_time, value_time)
    attended_back = to_space(attended_time)
    update_time = jnp.dot(attended_back, full_out_time, preferred_element_type=jnp.float32)
    frames_out = (stream.astype(jnp.float32) + update_time).astype(jnp.bfloat16)
    grad_att_time = jnp.dot(grad_out, full_out_time.T, preferred_element_type=jnp.float32).astype(
        jnp.bfloat16
    )
    grad_time_rows = to_frames(grad_att_time)
    gradients = time_back(
        query_time, key_time, value_time, attended_time, grad_time_rows, totals_time
    )
    grad_project_time = to_space(gradients)
    grad_normed_time = jnp.dot(
        grad_project_time, full_qkv_time.T, preferred_element_type=jnp.float32
    )
    grad_stream = (grad_out.astype(jnp.float32) + rms_back(stream, grad_normed_time)).astype(
        jnp.bfloat16
    )
    grad_attended = jnp.dot(
        grad_stream, full_out_space.T, preferred_element_type=jnp.float32
    ).astype(jnp.bfloat16)
    grad_query, key_partial, value_partial = space_back(
        queries, key_window, value_window, allowed, totals, attended, grad_attended
    )
    key_send = jnp.concatenate([key_partial[:shard], key_partial[2 * shard :]], axis=0).astype(
        jnp.bfloat16
    )
    value_send = jnp.concatenate(
        [value_partial[:shard], value_partial[2 * shard :]], axis=0
    ).astype(jnp.bfloat16)
    key_got, value_got = rim(key_send, value_send, shard)
    grad_key = (
        key_partial[shard : 2 * shard]
        + key_got[:shard].astype(jnp.float32)
        + key_got[3 * shard :].astype(jnp.float32)
    ).astype(jnp.bfloat16)
    grad_value = (
        value_partial[shard : 2 * shard]
        + value_got[:shard].astype(jnp.float32)
        + value_got[3 * shard :].astype(jnp.float32)
    ).astype(jnp.bfloat16)
    grad_project = jnp.concatenate([grad_query, grad_key, grad_value], axis=1)
    grad_normed = jnp.dot(grad_project, full_qkv_space.T, preferred_element_type=jnp.float32)
    grad_in = (grad_stream.astype(jnp.float32) + rms_back(local_in, grad_normed)).astype(
        jnp.bfloat16
    )
    return (frames_out[None], grad_in[None])


def solution(mesh):
    in_specs = (
        P(("dp", "frame"), "space", None),
        P(("dp", "frame"), "space", None),
        P("space", None),
        P("space", None),
        P("space", None),
        P("space", None),
        P(),
    )
    out_specs = (P(("dp", "frame"), "space", None), P(("dp", "frame"), "space", None))
    return jax.shard_map(local, mesh=mesh, in_specs=in_specs, out_specs=out_specs, check_vma=False)
```

profile of v0, /device:TPU:198, one launch (start us, length us, event | category | flops | bytes accessed | tf_op | source)
XLA Modules:
  0.0 301.4 jit_solution(5994388892875304705)
XLA Ops:
  7.2 1.7 pad_maximum_fusion.3
  9.3 1.0 fusion.55
  11.0 109.4 %all-gather.2.cloned.1.call-done = bf16[768,6144]{1,0:T(8,128)(2,1)} async-done(((bf16[24,6144]{1,0:T(8,128)(2,1)}), bf16[768,6144]{1,0:T(8,128)(2,1)}) %all-gather.2.cloned.1.call-update) | async-done | bytes 9437200 | tf_op jit(solution)/shard_map/all_gather | solution.py:214
  120.4 2.8 convolution_convert_fusion.1
  123.3 4.6 %collective-permute-start.2 = (bf16[128,768]{1,0:T(8,128)(2,1)S(1)}, bf16[128,768]{1,0:T(8,128)(2,1)S(1)}, u32[]{:S(2)}, u32[]{:S(2)}) collective-permute-start(bf16[128,768]{1,0:T(8,128)(2,1)S(1)} %get-tuple-element.27), channel_id=1, source_target_pairs={{0,2},{2,4},{4,6},{6,8},{8,10},{10,12},{12,14},{14,16},{16,18},{18... | collective-permute-start | bytes 589832 | tf_op jit(solution)/shard_map/ppermute | solution.py:20
  127.9 1.9 collective-permute-start.3
  129.9 7.2 %collective-permute-start = (bf16[128,768]{1,0:T(8,128)(2,1)S(1)}, bf16[128,768]{1,0:T(8,128)(2,1)S(1)}, u32[]{:S(2)}, u32[]{:S(2)}) collective-permute-start(bf16[128,768]{1,0:T(8,128)(2,1)S(1)} %get-tuple-element.28), channel_id=1, source_target_pairs={{0,2},{2,4},{4,6},{6,8},{8,10},{10,12},{12,14},{14,16},{16,18},{18... | collective-permute-start | bytes 589832 | tf_op jit(solution)/shard_map/ppermute | solution.py:20
  137.1 1.9 collective-permute-start.1
  139.8 1.8 fusion.43
  142.5 1.8 reduce.19
  145.0 6.7 %all-to-all-start.2 = ((bf16[8,2,6144]{2,1,0:T(2,128)(2,1)}), bf16[8,2,6144]{2,1,0:T(2,128)(2,1)S(1)}, u32[]{:S(2)}, u32[]{:S(2)}) async-start(bf16[8,2,6144]{2,1,0:T(2,128)(2,1)} %reshape.405), calls=%async_computation.2 | async-start | bytes 393216 | tf_op jit(solution)/shard_map/all_to_all | solution.py:198
  158.7 1.7 multiply_reduce_fusion.2
  160.4 2.7 fusion
  164.1 4.3 %reduce.20 = bf16[128,2304]{1,0:T(8,128)(2,1)S(1)} reduce(bf16[128,1,2304]{2,1,0:T(2,128)(2,1)S(1)} %bitcast.286, bf16[]{:T(256)} %broadcast.211), dimensions={1}, to_apply=%bitcast.285.reduce_sub_computation | reduce | bytes 1179650
  169.3 7.2 %all-to-all-start = ((bf16[8,2,18432]{2,1,0:T(2,128)(2,1)}), bf16[8,2,18432]{2,1,0:T(2,128)(2,1)S(1)}, u32[]{:S(2)}, u32[]{:S(2)}) async-start(bf16[8,2,18432]{2,1,0:T(2,128)(2,1)} %reshape.403), calls=%async_computation | async-start | bytes 1179648 | tf_op jit(solution)/shard_map/all_to_all | solution.py:198
  177.1 1.1 fusion.94
  178.2 1.1 fusion.96
  179.5 1.1 bitcast_reduce_fusion
  180.9 1.1 bitcast_convert_fusion
  182.0 11.6 %all-to-all-done = bf16[8,2,18432]{2,1,0:T(2,128)(2,1)S(1)} async-done(((bf16[8,2,18432]{2,1,0:T(2,128)(2,1)}), bf16[8,2,18432]{2,1,0:T(2,128)(2,1)S(1)}, u32[]{:S(2)}, u32[]{:S(2)}) %all-to-all-start) | async-done | bytes 589856 | tf_op jit(solution)/shard_map/all_to_all | solution.py:198
  195.4 1.3 fusion.8
  197.5 1.1 fusion.67
  198.6 3.4 %multiply_reduce_fusion = (f32[16,12,8]{2,1,0:T(8,128)S(1)}, bf16[16,12,64,8]{2,3,1,0:T(8,128)(2,1)}) fusion(f32[16,12,8,64]{3,1,0,2:T(8,128)} %bitcast_convert_fusion, f32[16,12,8,8]{2,3,1,0:T(8,128)} %copy-done.54, bf16[8,16,12,64]{3,2,1,0:T(8,128)(2,1)S(1)} %reshape.347), kind=kOutput, calls=%fused_computation.101 | convolution fusion | flops 1990663 | bytes 841728 | tf_op jit(solution)/shard_map/phfg,gphd->fphd/dot_general | solution.py:143
  202.0 1.7 fusion.10
  203.8 1.2 fusion.15
  205.4 2.0 fusion.13
  210.0 3.4 %all-to-all-start.1 = ((bf16[8,16,768]{2,1,0:T(8,128)(2,1)}), bf16[8,16,768]{2,1,0:T(8,128)(2,1)S(1)}, u32[]{:S(2)}, u32[]{:S(2)}) async-start(bf16[8,16,768]{2,1,0:T(8,128)(2,1)} %reshape.350), calls=%async_computation.1 | async-start | bytes 393216 | tf_op jit(solution)/shard_map/all_to_all | solution.py:202
  214.2 8.8 %all-to-all-done.1 = bf16[8,16,768]{2,1,0:T(8,128)(2,1)S(1)} async-done(((bf16[8,16,768]{2,1,0:T(8,128)(2,1)}), bf16[8,16,768]{2,1,0:T(8,128)(2,1)S(1)}, u32[]{:S(2)}, u32[]{:S(2)}) %all-to-all-start.1) | async-done | bytes 196640 | tf_op jit(solution)/shard_map/all_to_all | solution.py:202
  223.0 3.8 %all-to-all-start.3 = ((bf16[8,16,2304]{2,1,0:T(8,128)(2,1)}), bf16[8,16,2304]{2,1,0:T(8,128)(2,1)S(1)}, u32[]{:S(2)}, u32[]{:S(2)}) async-start(bf16[8,16,2304]{2,1,0:T(8,128)(2,1)} %pad_maximum_fusion.2), calls=%async_computation.3 | async-start | bytes 1179648 | tf_op jit(solution)/shard_map/all_to_all | solution.py:202
  228.4 1.1 fusion.88
  229.5 1.1 fusion.86
  230.6 2.3 fusion.44
  232.9 8.2 %all-to-all-done.3 = bf16[8,16,2304]{2,1,0:T(8,128)(2,1)S(1)} async-done(((bf16[8,16,2304]{2,1,0:T(8,128)(2,1)}), bf16[8,16,2304]{2,1,0:T(8,128)(2,1)S(1)}, u32[]{:S(2)}, u32[]{:S(2)}) %all-to-all-start.3) | async-done | bytes 589856 | tf_op jit(solution)/shard_map/all_to_all | solution.py:202
  241.1 3.4 %multiply_reduce_fusion.1 = (f32[128]{0:T(128)S(1)}, f32[128,768]{1,0:T(8,128)S(1)}) fusion(f32[128,768]{1,0:T(8,128)S(1)} %get-tuple-element.40, bf16[128,2304]{1,0:T(8,128)(2,1)S(1)} %bitcast.315, bf16[768,6144]{1,0:T(8,128)(2,1)} %all-gather.2.cloned.1.call-done), kind=kOutput, calls=%fused_computation.120 | convolution fusion | flops 453181312 | bytes 4915712 | tf_op jit(solution)/shard_map/dot_general | solution.py:257
  244.7 1.8 convolution_convert_fusion.4
  247.3 2.1 fusion.98
  250.3 2.1 fusion.101
  253.2 1.4 fusion.104
  255.5 1.4 fusion.107
  257.7 1.5 fusion.110
  260.1 1.4 fusion.113
  263.0 6.7 %collective-permute-start.6 = (bf16[128,768]{0,1:T(8,128)(2,1)S(1)}, bf16[128,768]{0,1:T(8,128)(2,1)S(1)}, u32[]{:S(2)}, u32[]{:S(2)}) collective-permute-start(bf16[128,768]{0,1:T(8,128)(2,1)S(1)} %get-tuple-element.2), channel_id=1, source_target_pairs={{0,2},{2,4},{4,6},{6,8},{8,10},{10,12},{12,14},{14,16},{16,18},{18... | collective-permute-start | bytes 589832 | tf_op jit(solution)/shard_map/ppermute | solution.py:20
  269.7 1.9 collective-permute-start.7
  271.9 7.2 %collective-permute-start.4 = (bf16[128,768]{0,1:T(8,128)(2,1)S(1)}, bf16[128,768]{0,1:T(8,128)(2,1)S(1)}, u32[]{:S(2)}, u32[]{:S(2)}) collective-permute-start(bf16[128,768]{0,1:T(8,128)(2,1)S(1)} %get-tuple-element.4), channel_id=1, source_target_pairs={{0,2},{2,4},{4,6},{6,8},{8,10},{10,12},{12,14},{14,16},{16,18},{18... | collective-permute-start | bytes 589832 | tf_op jit(solution)/shard_map/ppermute | solution.py:20
  279.1 1.9 collective-permute-start.5
  281.1 1.1 collective-permute-done.4
  282.3 7.7 %collective-permute-done.5 = bf16[128,768]{0,1:T(8,128)(2,1)S(1)} collective-permute-done((bf16[128,768]{0,1:T(8,128)(2,1)S(1)}, bf16[128,768]{0,1:T(8,128)(2,1)S(1)}, u32[]{:S(2)}, u32[]{:S(2)}) %collective-permute-start.5) | collective-permute-done | bytes 196640 | tf_op jit(solution)/shard_map/ppermute | solution.py:22
  290.2 3.4 %fusion.61 = (f32[128]{0:T(128)S(1)}, f32[128,768]{1,0:T(8,128)S(1)}) fusion(bf16[1,128,768]{2,1,0:T(8,128)(2,1)S(1)} %copy-done.1, bf16[128,2304]{0,1:T(8,128)(2,1)S(1)} %fusion.77, bf16[768,6144]{1,0:T(8,128)(2,1)} %all-gather.2.cloned.1.call-done), kind=kOutput, calls=%fused_computation.112 | convolution fusion | flops 453279616 | bytes 4719104 | tf_op jit(solution)/shard_map/dot_general | solution.py:287
  (252 shorter events, 28.3 us)
Async XLA Ops:
  7.2 1.8 copy-start
  7.2 113.2 %all-gather.2.cloned.1.call-start = ((), (), s32[]{:S(2)}) async-start(), calls=%async_computation.4 | async-start | bytes 9732096 | tf_op jit(solution)/shard_map/all_gather | solution.py:214
  11.0 109.4 %copy-start.52 = (f32[128]{0:T(128)}, f32[128]{0:T(128)S(1)}, u32[]{:S(2)}) copy-start(f32[128]{0:T(128)S(1)} %get-tuple-element.36) | copy-start | bytes 1540
  123.2 16.6 %copy-start.34 = (bf16[1,128,768]{2,1,0:T(8,128)(2,1)S(1)}, bf16[1,128,768]{2,1,0:T(8,128)(2,1)}, u32[]{:S(2)}) copy-start(bf16[1,128,768]{2,1,0:T(8,128)(2,1)} %param.8) | copy-start | bytes 589828
  123.3 28.5 %collective-permute-start.2 = (bf16[128,768]{1,0:T(8,128)(2,1)S(1)}, bf16[128,768]{1,0:T(8,128)(2,1)S(1)}, u32[]{:S(2)}, u32[]{:S(2)}) collective-permute-start(bf16[128,768]{1,0:T(8,128)(2,1)S(1)} %get-tuple-element.27), channel_id=1, source_target_pairs={{0,2},{2,4},{4,6},{6,8},{8,10},{10,12},{12,14},{14,16},{16,18},{18... | collective-permute-start | bytes 589832 | tf_op jit(solution)/shard_map/ppermute | solution.py:20
  127.9 23.9 %collective-permute-start.3 = (bf16[128,768]{1,0:T(8,128)(2,1)S(1)}, bf16[128,768]{1,0:T(8,128)(2,1)S(1)}, u32[]{:S(2)}, u32[]{:S(2)}) collective-permute-start(bf16[128,768]{1,0:T(8,128)(2,1)S(1)} %get-tuple-element.27), channel_id=1, source_target_pairs={{2,0},{4,2},{6,4},{8,6},{10,8},{12,10},{14,12},{16,14},{18,16},{20... | collective-permute-start | bytes 589832 | tf_op jit(solution)/shard_map/ppermute | solution.py:22
  129.9 22.2 %collective-permute-start = (bf16[128,768]{1,0:T(8,128)(2,1)S(1)}, bf16[128,768]{1,0:T(8,128)(2,1)S(1)}, u32[]{:S(2)}, u32[]{:S(2)}) collective-permute-start(bf16[128,768]{1,0:T(8,128)(2,1)S(1)} %get-tuple-element.28), channel_id=1, source_target_pairs={{0,2},{2,4},{4,6},{6,8},{8,10},{10,12},{12,14},{14,16},{16,18},{18... | collective-permute-start | bytes 589832 | tf_op jit(solution)/shard_map/ppermute | solution.py:20
  137.1 15.0 %collective-permute-start.1 = (bf16[128,768]{1,0:T(8,128)(2,1)S(1)}, bf16[128,768]{1,0:T(8,128)(2,1)S(1)}, u32[]{:S(2)}, u32[]{:S(2)}) collective-permute-start(bf16[128,768]{1,0:T(8,128)(2,1)S(1)} %get-tuple-element.28), channel_id=1, source_target_pairs={{2,0},{4,2},{6,4},{8,6},{10,8},{12,10},{14,12},{16,14},{18,16},{20... | collective-permute-start | bytes 589832 | tf_op jit(solution)/shard_map/ppermute | solution.py:22
  139.4 16.0 %copy-start.26 = (bf16[128,128]{0,1:T(8,128)(2,1)}, bf16[128,128]{0,1:T(8,128)(2,1)S(1)}, u32[]{:S(2)}) copy-start(bf16[128,128]{0,1:T(8,128)(2,1)S(1)} %copy.191) | copy-start | bytes 98308
  139.5 16.5 %copy-start.28 = (bf16[128,128]{0,1:T(8,128)(2,1)}, bf16[128,128]{0,1:T(8,128)(2,1)S(1)}, u32[]{:S(2)}) copy-start(bf16[128,128]{0,1:T(8,128)(2,1)S(1)} %copy.194) | copy-start | bytes 98308
  139.7 17.0 %copy-start.30 = (bf16[128,128]{0,1:T(8,128)(2,1)}, bf16[128,128]{0,1:T(8,128)(2,1)S(1)}, u32[]{:S(2)}) copy-start(bf16[128,128]{0,1:T(8,128)(2,1)S(1)} %copy.197) | copy-start | bytes 98308
  139.8 17.8 %copy-start.32 = (bf16[128,128]{0,1:T(8,128)(2,1)}, bf16[128,128]{0,1:T(8,128)(2,1)S(1)}, u32[]{:S(2)}) copy-start(bf16[128,128]{0,1:T(8,128)(2,1)S(1)} %copy.200) | copy-start | bytes 98308
  145.0 24.3 %all-to-all-start.2 = ((bf16[8,2,6144]{2,1,0:T(2,128)(2,1)}), bf16[8,2,6144]{2,1,0:T(2,128)(2,1)S(1)}, u32[]{:S(2)}, u32[]{:S(2)}) async-start(bf16[8,2,6144]{2,1,0:T(2,128)(2,1)} %reshape.405), calls=%async_computation.2 | async-start | bytes 393216 | tf_op jit(solution)/shard_map/all_to_all | solution.py:198
  152.4 2.7 copy-start.16
  154.2 2.1 copy-start.20
  154.5 2.5 copy-start.22
  154.8 3.1 %copy-start.24 = (bf16[384,128]{0,1:T(8,128)(2,1)}, bf16[384,128]{0,1:T(8,128)(2,1)S(1)}, u32[]{:S(2)}) copy-start(bf16[384,128]{0,1:T(8,128)(2,1)S(1)} %copy.199) | copy-start | bytes 294916
  157.6 2.8 copy-start.47
  158.2 4.9 %copy-start.49 = (bf16[2,64,128]{2,1,0:T(8,128)(2,1)}, bf16[2,64,128]{2,1,0:T(8,128)(2,1)S(1)}, u32[]{:S(2)}) copy-start(bf16[2,64,128]{2,1,0:T(8,128)(2,1)S(1)} %convolution_convert_fusion.6) | copy-start | bytes 98308
  169.3 24.3 %all-to-all-start = ((bf16[8,2,18432]{2,1,0:T(2,128)(2,1)}), bf16[8,2,18432]{2,1,0:T(2,128)(2,1)S(1)}, u32[]{:S(2)}, u32[]{:S(2)}) async-start(bf16[8,2,18432]{2,1,0:T(2,128)(2,1)} %reshape.403), calls=%async_computation | async-start | bytes 1179648 | tf_op jit(solution)/shard_map/all_to_all | solution.py:198
  205.4 2.0 copy-start.2
  210.0 13.1 %all-to-all-start.1 = ((bf16[8,16,768]{2,1,0:T(8,128)(2,1)}), bf16[8,16,768]{2,1,0:T(8,128)(2,1)S(1)}, u32[]{:S(2)}, u32[]{:S(2)}) async-start(bf16[8,16,768]{2,1,0:T(8,128)(2,1)} %reshape.350), calls=%async_computation.1 | async-start | bytes 393216 | tf_op jit(solution)/shard_map/all_to_all | solution.py:202
  213.4 13.5 %copy-start.27 = (bf16[128,128]{0,1:T(8,128)(2,1)S(1)}, bf16[128,128]{0,1:T(8,128)(2,1)}, u32[]{:S(2)}) copy-start(bf16[128,128]{0,1:T(8,128)(2,1)} %copy-done.26) | copy-start | bytes 98308
  223.0 18.1 %all-to-all-start.3 = ((bf16[8,16,2304]{2,1,0:T(8,128)(2,1)}), bf16[8,16,2304]{2,1,0:T(8,128)(2,1)S(1)}, u32[]{:S(2)}, u32[]{:S(2)}) async-start(bf16[8,16,2304]{2,1,0:T(8,128)(2,1)} %pad_maximum_fusion.2), calls=%async_computation.3 | async-start | bytes 1179648 | tf_op jit(solution)/shard_map/all_to_all | solution.py:202
  241.1 3.4 %copy-start.35 = (bf16[1,128,768]{2,1,0:T(8,128)(2,1)S(1)}, bf16[1,128,768]{2,1,0:T(8,128)(2,1)}, u32[]{:S(2)}) copy-start(bf16[1,128,768]{2,1,0:T(8,128)(2,1)} %param.8) | copy-start | bytes 589828
  244.7 2.6 copy-start.50
  246.5 2.9 copy-start.13
  246.5 2.9 copy-start.25
  247.3 2.9 copy-start.48
  249.7 2.6 copy-start.12
  249.7 2.6 copy-start.23
  250.3 2.9 copy-start.46
  252.6 2.0 copy-start.21
  253.2 2.2 copy-start.44
  254.9 2.0 copy-start.19
  255.5 2.2 copy-start.42
  257.1 2.1 copy-start.11
  257.1 2.1 copy-start.17
  257.7 2.2 copy-start.38
  257.7 2.3 copy-start.40
  259.5 2.0 copy-start.10
  259.5 2.0 copy-start.15
  263.0 27.1 %collective-permute-start.6 = (bf16[128,768]{0,1:T(8,128)(2,1)S(1)}, bf16[128,768]{0,1:T(8,128)(2,1)S(1)}, u32[]{:S(2)}, u32[]{:S(2)}) collective-permute-start(bf16[128,768]{0,1:T(8,128)(2,1)S(1)} %get-tuple-element.2), channel_id=1, source_target_pairs={{0,2},{2,4},{4,6},{6,8},{8,10},{10,12},{12,14},{14,16},{16,18},{18... | collective-permute-start | bytes 589832 | tf_op jit(solution)/shard_map/ppermute | solution.py:20
  269.7 20.4 %collective-permute-start.7 = (bf16[128,768]{0,1:T(8,128)(2,1)S(1)}, bf16[128,768]{0,1:T(8,128)(2,1)S(1)}, u32[]{:S(2)}, u32[]{:S(2)}) collective-permute-start(bf16[128,768]{0,1:T(8,128)(2,1)S(1)} %get-tuple-element.3), channel_id=1, source_target_pairs={{2,0},{4,2},{6,4},{8,6},{10,8},{12,10},{14,12},{16,14},{18,16},{20... | collective-permute-start | bytes 589832 | tf_op jit(solution)/shard_map/ppermute | solution.py:22
  271.9 10.4 %collective-permute-start.4 = (bf16[128,768]{0,1:T(8,128)(2,1)S(1)}, bf16[128,768]{0,1:T(8,128)(2,1)S(1)}, u32[]{:S(2)}, u32[]{:S(2)}) collective-permute-start(bf16[128,768]{0,1:T(8,128)(2,1)S(1)} %get-tuple-element.4), channel_id=1, source_target_pairs={{0,2},{2,4},{4,6},{6,8},{8,10},{10,12},{12,14},{14,16},{16,18},{18... | collective-permute-start | bytes 589832 | tf_op jit(solution)/shard_map/ppermute | solution.py:20
  279.1 10.9 %collective-permute-start.5 = (bf16[128,768]{0,1:T(8,128)(2,1)S(1)}, bf16[128,768]{0,1:T(8,128)(2,1)S(1)}, u32[]{:S(2)}, u32[]{:S(2)}) collective-permute-start(bf16[128,768]{0,1:T(8,128)(2,1)S(1)} %get-tuple-element.5), channel_id=1, source_target_pairs={{2,0},{4,2},{6,4},{8,6},{10,8},{12,10},{14,12},{16,14},{18,16},{20... | collective-permute-start | bytes 589832 | tf_op jit(solution)/shard_map/ppermute | solution.py:22
  290.2 3.4 %copy-start.51 = (f32[128]{0:T(128)S(1)}, f32[128]{0:T(128)}, u32[]{:S(2)}) copy-start(f32[128]{0:T(128)} %get-tuple-element.35) | copy-start | bytes 1540
  290.2 3.4 %copy-start.53 = (f32[128]{0:T(128)S(1)}, f32[128]{0:T(128)}, u32[]{:S(2)}) copy-start(f32[128]{0:T(128)} %copy-done.52) | copy-start | bytes 1540
  (20 other events, 20.1 us)
Sparse Core Ops, SparseCore 0:
  11.2 109.1 all-gather.1
where the time goes:
time: 303 us; the launch traced here: 301 us
  waiting for transfers between devices  147 us (49%)
  starting transfers between devices  54.6 us (18%)
  matrix products  52 us (17%)
  local copies, waits for them, and re-layouts  17.4 us (6%)
  between operations  15.7 us (5%)
  other arithmetic  14.7 us (5%)
    all_gather x1, waiting for transfers between devices, local(): all_weights = lax.all_gather(weight_rows, 'space', axis=0, tiled=True)  109 us
    ppermute x4, starting transfers between devices, padded(): lax.ppermute(tail, axis, [(i, (i + 1) % count) for i in range(ends)])  25.8 us
    all_to_all x2, waiting for transfers between devices, to_space(): lax.all_to_all(frame_rows, 'frame', split_axis=0, concat_axis=1, tiled=True)  17 us
    all_to_all x2, starting transfers between devices, to_frames(): lax.all_to_all(local_rows[None], 'frame', split_axis=1, concat_axis=0, ti...  13.9 us
    all_to_all x2, waiting for transfers between devices, to_frames(): lax.all_to_all(local_rows[None], 'frame', split_axis=1, concat_axis=0, ti...  11.6 us
    dot_general x6, matrix products, space_back(): jnp.einsum('gst,sgh->tgh', probability, grad_part, preferred_element_type...  9.81 us
    ppermute x4, waiting for transfers between devices, padded(): lax.ppermute(head, axis, [((i + 1) % count, i) for i in range(ends)])  7.72 us
    ppermute x4, starting transfers between devices, padded(): lax.ppermute(head, axis, [((i + 1) % count, i) for i in range(ends)])  7.68 us
  transfers between devices with their start and end apart: 13, of which 6 were waited for; matrix products, arithmetic and copies ran while one was open for 12% of the time, Pallas kernels for 0%

commit v1 on v0

--- a/solution.py
+++ b/solution.py
@@ -211,7 +211,10 @@
     grad_out = cotangent[0]
     shard, feature_count = local_in.shape
     weight_rows = jnp.concatenate([w_qkv_space, w_out_space, w_qkv_time, w_out_time], axis=1)
-    all_weights = lax.all_gather(weight_rows, "space", axis=0, tiled=True)
+    count_2 = lax.axis_size("space")
+    blocks = jnp.stack([weight_rows for _ in range(count_2)])
+    blocks = lax.all_to_all(blocks, "space", split_axis=0, concat_axis=0)
+    all_weights = jnp.concatenate(blocks, axis=0)
     widths = [w_qkv_space.shape[1], w_out_space.shape[1], w_qkv_time.shape[1], w_out_time.shape[1]]
     bounds = [0]
     for width in widths:

time: 303 us -> 417 us (1.38)
  waiting for transfers between devices: 147 us -> 262 us
  between operations: 15.7 us -> 2.36 us
  starting transfers between devices: 54.6 us -> 63.2 us
    all_to_all x0 -> x1, waiting for transfers between devices: none -> 223 us  [local(): blocks = lax.all_to_all(blocks, 'space', split_axis=0, concat_axis=0)]
    all_gather x1 -> x0, waiting for transfers between devices: 109 us -> none  [local(): all_weights = lax.all_gather(weight_rows, 'space', axis=0, tiled=True)]
    all_to_all x0 -> x1, starting transfers between devices: none -> 10.9 us  [local(): blocks = lax.all_to_all(blocks, 'space', split_axis=0, concat_axis=0)]
    another operation x0 -> x1, local copies, waits for them, and re-layouts: none -> 4.82 us  [local(): blocks = jnp.stack([weight_rows for _ in range(count_2)])]
    ppermute x4, starting transfers between devices: 25.8 us -> 21.1 us  [padded(): lax.ppermute(tail, axis, [(i, (i + 1) % count) for i in range(ends)])]
  transfers between devices with their start and end apart: 13 -> 13, of which waited for: 6 -> 6; matrix products, arithmetic and copies ran while one was open for 12% -> 8% of each run, Pallas kernels for 0% -> 0%
where the time goes in v1:
time: 417 us; the launch traced here: 416 us
  waiting for transfers between devices  262 us (63%)
  starting transfers between devices  63.2 us (15%)
  matrix products  54.2 us (13%)
  local copies, waits for them, and re-layouts  21 us (5%)
  other arithmetic  13.2 us (3%)
    all_to_all x1, waiting for transfers between devices, local(): blocks = lax.all_to_all(blocks, 'space', split_axis=0, concat_axis=0)  223 us
    ppermute x4, starting transfers between devices, padded(): lax.ppermute(tail, axis, [(i, (i + 1) % count) for i in range(ends)])  21.1 us
    all_to_all x2, waiting for transfers between devices, to_space(): lax.all_to_all(frame_rows, 'frame', split_axis=0, concat_axis=1, tiled=True)  18.4 us
    all_to_all x2, starting transfers between devices, to_frames(): lax.all_to_all(local_rows[None], 'frame', split_axis=1, concat_axis=0, ti...  14.3 us
    all_to_all x2, waiting for transfers between devices, to_frames(): lax.all_to_all(local_rows[None], 'frame', split_axis=1, concat_axis=0, ti...  12 us
    all_to_all x1, starting transfers between devices, local(): blocks = lax.all_to_all(blocks, 'space', split_axis=0, concat_axis=0)  10.9 us
    dot_general x6, matrix products, space_back(): jnp.einsum('gst,sgh->tgh', probability, grad_part, preferred_element_type...  9.78 us
    ppermute x4, starting transfers between devices, padded(): lax.ppermute(head, axis, [((i + 1) % count, i) for i in range(ends)])  9.68 us
  transfers between devices with their start and end apart: 13, of which 6 were waited for; matrix products, arithmetic and copies ran while one was open for 8% of the time, Pallas kernels for 0%

profile of v1, /device:TPU:198, one launch (start us, length us, event | category | flops | bytes accessed | tf_op | source)
XLA Modules:
  0.0 415.8 jit_solution(6289985336670856458)
XLA Ops:
  0.6 1.0 pad_maximum_fusion.3
  1.7 4.8 %stack.2 = bf16[32,24,6144]{2,1,0:T(8,128)(2,1)} broadcast(bf16[24,6144]{1,0:T(8,128)(2,1)S(1)} %pad_maximum_fusion.3), dimensions={1,2} | broadcast | bytes 9732096 | tf_op jit(solution)/shard_map/stack | solution.py:215
  6.5 10.9 %all-to-all-start = ((bf16[32,24,6144]{2,1,0:T(8,128)(2,1)}), bf16[32,24,6144]{2,1,0:T(8,128)(2,1)}, u32[]{:S(2)}, u32[]{:S(2)}) async-start(bf16[32,24,6144]{2,1,0:T(8,128)(2,1)} %stack.2), calls=%async_computation | async-start | bytes 18874368 | tf_op jit(solution)/shard_map/all_to_all | solution.py:216
  18.4 222.7 %all-to-all-done = bf16[32,24,6144]{2,1,0:T(8,128)(2,1)} async-done(((bf16[32,24,6144]{2,1,0:T(8,128)(2,1)}), bf16[32,24,6144]{2,1,0:T(8,128)(2,1)}, u32[]{:S(2)}, u32[]{:S(2)}) %all-to-all-start) | async-done | bytes 9437216 | tf_op jit(solution)/shard_map/all_to_all | solution.py:216
  241.1 2.7 convolution_convert_fusion.1
  243.8 2.1 collective-permute-start.2
  245.9 3.9 collective-permute-start.3
  249.9 5.2 %collective-permute-start = (bf16[128,768]{1,0:T(8,128)(2,1)S(1)}, bf16[128,768]{1,0:T(8,128)(2,1)S(1)}, u32[]{:S(2)}, u32[]{:S(2)}) collective-permute-start(bf16[128,768]{1,0:T(8,128)(2,1)S(1)} %get-tuple-element.28), channel_id=1, source_target_pairs={{0,2},{2,4},{4,6},{6,8},{8,10},{10,12},{12,14},{14,16},{16,18},{18... | collective-permute-start | bytes 589832 | tf_op jit(solution)/shard_map/ppermute | solution.py:20
  255.1 1.9 collective-permute-start.1
  257.8 1.8 fusion.43
  260.6 1.8 reduce.19
  263.2 7.1 %all-to-all-start.3 = ((bf16[8,2,6144]{2,1,0:T(2,128)(2,1)}), bf16[8,2,6144]{2,1,0:T(2,128)(2,1)S(1)}, u32[]{:S(2)}, u32[]{:S(2)}) async-start(bf16[8,2,6144]{2,1,0:T(2,128)(2,1)} %reshape.411), calls=%async_computation.3 | async-start | bytes 393216 | tf_op jit(solution)/shard_map/all_to_all | solution.py:198
  277.4 1.7 multiply_reduce_fusion.2
  279.2 2.7 fusion
  282.8 4.3 %reduce.20 = bf16[128,2304]{1,0:T(8,128)(2,1)S(1)} reduce(bf16[128,1,2304]{2,1,0:T(2,128)(2,1)S(1)} %bitcast.287, bf16[]{:T(256)} %broadcast.213), dimensions={1}, to_apply=%bitcast.286.reduce_sub_computation | reduce | bytes 1179650
  288.1 7.2 %all-to-all-start.1 = ((bf16[8,2,18432]{2,1,0:T(2,128)(2,1)}), bf16[8,2,18432]{2,1,0:T(2,128)(2,1)S(1)}, u32[]{:S(2)}, u32[]{:S(2)}) async-start(bf16[8,2,18432]{2,1,0:T(2,128)(2,1)} %reshape.409), calls=%async_computation.1 | async-start | bytes 1179648 | tf_op jit(solution)/shard_map/all_to_all | solution.py:198
  295.9 1.1 fusion.86
  297.0 1.1 fusion.88
  298.3 1.1 bitcast_reduce_fusion
  299.8 1.1 bitcast_convert_fusion
  300.8 12.0 %all-to-all-done.1 = bf16[8,2,18432]{2,1,0:T(2,128)(2,1)S(1)} async-done(((bf16[8,2,18432]{2,1,0:T(2,128)(2,1)}), bf16[8,2,18432]{2,1,0:T(2,128)(2,1)S(1)}, u32[]{:S(2)}, u32[]{:S(2)}) %all-to-all-start.1) | async-done | bytes 589856 | tf_op jit(solution)/shard_map/all_to_all | solution.py:198
  314.5 1.3 fusion.8
  316.7 1.1 fusion.67
  317.8 3.4 multiply_reduce_fusion
  321.2 1.7 fusion.10
  323.8 2.7 fusion.13
  329.1 3.4 all-to-all-start.2
  333.4 8.8 %all-to-all-done.2 = bf16[8,16,768]{2,1,0:T(8,128)(2,1)S(1)} async-done(((bf16[8,16,768]{2,1,0:T(8,128)(2,1)}), bf16[8,16,768]{2,1,0:T(8,128)(2,1)S(1)}, u32[]{:S(2)}, u32[]{:S(2)}) %all-to-all-start.2) | async-done | bytes 196640 | tf_op jit(solution)/shard_map/all_to_all | solution.py:202
  342.2 3.8 all-to-all-start.4
  346.0 1.1 fusion.90
  347.1 1.1 fusion.92
  349.0 2.3 fusion.44
  351.2 9.6 %all-to-all-done.4 = bf16[8,16,2304]{2,1,0:T(8,128)(2,1)S(1)} async-done(((bf16[8,16,2304]{2,1,0:T(8,128)(2,1)}), bf16[8,16,2304]{2,1,0:T(8,128)(2,1)S(1)}, u32[]{:S(2)}, u32[]{:S(2)}) %all-to-all-start.4) | async-done | bytes 589856 | tf_op jit(solution)/shard_map/all_to_all | solution.py:202
  360.8 3.4 multiply_reduce_fusion.1
  364.4 1.8 convolution_convert_fusion.4
  366.5 1.4 fusion.98
  369.3 2.1 fusion.101
  372.9 1.4 fusion.104
  375.7 2.1 fusion.107
  379.2 1.5 fusion.110
  381.6 1.4 fusion.113
  384.3 6.6 %collective-permute-start.6 = (bf16[128,768]{0,1:T(8,128)(2,1)S(1)}, bf16[128,768]{0,1:T(8,128)(2,1)S(1)}, u32[]{:S(2)}, u32[]{:S(2)}) collective-permute-start(bf16[128,768]{0,1:T(8,128)(2,1)S(1)} %get-tuple-element.2), channel_id=1, source_target_pairs={{0,2},{2,4},{4,6},{6,8},{8,10},{10,12},{12,14},{14,16},{16,18},{18... | collective-permute-start | bytes 589832 | tf_op jit(solution)/shard_map/ppermute | solution.py:20
  390.9 1.9 collective-permute-start.7
  393.2 7.2 %collective-permute-start.4 = (bf16[128,768]{0,1:T(8,128)(2,1)S(1)}, bf16[128,768]{0,1:T(8,128)(2,1)S(1)}, u32[]{:S(2)}, u32[]{:S(2)}) collective-permute-start(bf16[128,768]{0,1:T(8,128)(2,1)S(1)} %get-tuple-element.4), channel_id=1, source_target_pairs={{0,2},{2,4},{4,6},{6,8},{8,10},{10,12},{12,14},{14,16},{16,18},{18... | collective-permute-start | bytes 589832 | tf_op jit(solution)/shard_map/ppermute | solution.py:20
  400.4 1.9 collective-permute-start.5
  402.5 1.1 collective-permute-done.4
  403.6 7.7 %collective-permute-done.5 = bf16[128,768]{0,1:T(8,128)(2,1)S(1)} collective-permute-done((bf16[128,768]{0,1:T(8,128)(2,1)S(1)}, bf16[128,768]{0,1:T(8,128)(2,1)S(1)}, u32[]{:S(2)}, u32[]{:S(2)}) %collective-permute-start.5) | collective-permute-done | bytes 196640 | tf_op jit(solution)/shard_map/ppermute | solution.py:22
  411.5 3.4 fusion.61
  (262 shorter events, 30.0 us)
Async XLA Ops:
  0.6 16.7 %copy-start = (s32[32,4]{0,1:T(4,128)S(1)}, s32[32,4]{0,1:T(4,128)}, u32[]{:S(2)}) copy-start(s32[32,4]{0,1:T(4,128)} %param.13) | copy-start | bytes 1540
  6.5 11.2 %copy-start.1 = (bf16[1,128,768]{2,1,0:T(8,128)(2,1)S(1)}, bf16[1,128,768]{2,1,0:T(8,128)(2,1)}, u32[]{:S(2)}) copy-start(bf16[1,128,768]{2,1,0:T(8,128)(2,1)} %param.7) | copy-start | bytes 589828
  6.5 234.6 %all-to-all-start = ((bf16[32,24,6144]{2,1,0:T(8,128)(2,1)}), bf16[32,24,6144]{2,1,0:T(8,128)(2,1)}, u32[]{:S(2)}, u32[]{:S(2)}) async-start(bf16[32,24,6144]{2,1,0:T(8,128)(2,1)} %stack.2), calls=%async_computation | async-start | bytes 18874368 | tf_op jit(solution)/shard_map/all_to_all | solution.py:216
  18.4 222.7 %copy-start.57 = (f32[128]{0:T(128)}, f32[128]{0:T(128)S(1)}, u32[]{:S(2)}) copy-start(f32[128]{0:T(128)S(1)} %get-tuple-element.36) | copy-start | bytes 1540
  243.8 14.0 %copy-start.36 = (bf16[1,128,768]{2,1,0:T(8,128)(2,1)S(1)}, bf16[1,128,768]{2,1,0:T(8,128)(2,1)}, u32[]{:S(2)}) copy-start(bf16[1,128,768]{2,1,0:T(8,128)(2,1)} %param.8) | copy-start | bytes 589828
  243.8 26.4 %collective-permute-start.2 = (bf16[128,768]{1,0:T(8,128)(2,1)S(1)}, bf16[128,768]{1,0:T(8,128)(2,1)S(1)}, u32[]{:S(2)}, u32[]{:S(2)}) collective-permute-start(bf16[128,768]{1,0:T(8,128)(2,1)S(1)} %get-tuple-element.27), channel_id=1, source_target_pairs={{0,2},{2,4},{4,6},{6,8},{8,10},{10,12},{12,14},{14,16},{16,18},{18... | collective-permute-start | bytes 589832 | tf_op jit(solution)/shard_map/ppermute | solution.py:20
  245.9 24.4 %collective-permute-start.3 = (bf16[128,768]{1,0:T(8,128)(2,1)S(1)}, bf16[128,768]{1,0:T(8,128)(2,1)S(1)}, u32[]{:S(2)}, u32[]{:S(2)}) collective-permute-start(bf16[128,768]{1,0:T(8,128)(2,1)S(1)} %get-tuple-element.27), channel_id=1, source_target_pairs={{2,0},{4,2},{6,4},{8,6},{10,8},{12,10},{14,12},{16,14},{18,16},{20... | collective-permute-start | bytes 589832 | tf_op jit(solution)/shard_map/ppermute | solution.py:22
  249.9 20.7 %collective-permute-start = (bf16[128,768]{1,0:T(8,128)(2,1)S(1)}, bf16[128,768]{1,0:T(8,128)(2,1)S(1)}, u32[]{:S(2)}, u32[]{:S(2)}) collective-permute-start(bf16[128,768]{1,0:T(8,128)(2,1)S(1)} %get-tuple-element.28), channel_id=1, source_target_pairs={{0,2},{2,4},{4,6},{6,8},{8,10},{10,12},{12,14},{14,16},{16,18},{18... | collective-permute-start | bytes 589832 | tf_op jit(solution)/shard_map/ppermute | solution.py:20
  255.1 15.5 %collective-permute-start.1 = (bf16[128,768]{1,0:T(8,128)(2,1)S(1)}, bf16[128,768]{1,0:T(8,128)(2,1)S(1)}, u32[]{:S(2)}, u32[]{:S(2)}) collective-permute-start(bf16[128,768]{1,0:T(8,128)(2,1)S(1)} %get-tuple-element.28), channel_id=1, source_target_pairs={{2,0},{4,2},{6,4},{8,6},{10,8},{12,10},{14,12},{16,14},{18,16},{20... | collective-permute-start | bytes 589832 | tf_op jit(solution)/shard_map/ppermute | solution.py:22
  257.4 17.1 %copy-start.26 = (bf16[128,128]{0,1:T(8,128)(2,1)}, bf16[128,128]{0,1:T(8,128)(2,1)S(1)}, u32[]{:S(2)}) copy-start(bf16[128,128]{0,1:T(8,128)(2,1)S(1)} %copy.191) | copy-start | bytes 98308
  257.5 17.6 %copy-start.28 = (bf16[128,128]{0,1:T(8,128)(2,1)}, bf16[128,128]{0,1:T(8,128)(2,1)S(1)}, u32[]{:S(2)}) copy-start(bf16[128,128]{0,1:T(8,128)(2,1)S(1)} %copy.194) | copy-start | bytes 98308
  257.7 18.1 %copy-start.30 = (bf16[128,128]{0,1:T(8,128)(2,1)}, bf16[128,128]{0,1:T(8,128)(2,1)S(1)}, u32[]{:S(2)}) copy-start(bf16[128,128]{0,1:T(8,128)(2,1)S(1)} %copy.197) | copy-start | bytes 98308
  257.8 18.6 %copy-start.33 = (bf16[128,128]{0,1:T(8,128)(2,1)}, bf16[128,128]{0,1:T(8,128)(2,1)S(1)}, u32[]{:S(2)}) copy-start(bf16[128,128]{0,1:T(8,128)(2,1)S(1)} %copy.200) | copy-start | bytes 98308
  263.2 25.0 %all-to-all-start.3 = ((bf16[8,2,6144]{2,1,0:T(2,128)(2,1)}), bf16[8,2,6144]{2,1,0:T(2,128)(2,1)S(1)}, u32[]{:S(2)}, u32[]{:S(2)}) async-start(bf16[8,2,6144]{2,1,0:T(2,128)(2,1)} %reshape.411), calls=%async_computation.3 | async-start | bytes 393216 | tf_op jit(solution)/shard_map/all_to_all | solution.py:198
  270.9 2.7 copy-start.16
  272.8 2.7 copy-start.20
  273.0 3.0 copy-start.22
  273.3 3.4 copy-start.24
  276.4 2.8 copy-start.52
  277.0 4.9 %copy-start.54 = (bf16[2,64,128]{2,1,0:T(8,128)(2,1)}, bf16[2,64,128]{2,1,0:T(8,128)(2,1)S(1)}, u32[]{:S(2)}) copy-start(bf16[2,64,128]{2,1,0:T(8,128)(2,1)S(1)} %convolution_convert_fusion.6) | copy-start | bytes 98308
  287.2 8.8 %copy-start.34 = (bf16[128,128]{0,1:T(8,128)(2,1)S(1)}, bf16[128,128]{0,1:T(8,128)(2,1)}, u32[]{:S(2)}) copy-start(bf16[128,128]{0,1:T(8,128)(2,1)} %copy-done.33) | copy-start | bytes 98308
  288.1 24.7 %all-to-all-start.1 = ((bf16[8,2,18432]{2,1,0:T(2,128)(2,1)}), bf16[8,2,18432]{2,1,0:T(2,128)(2,1)S(1)}, u32[]{:S(2)}, u32[]{:S(2)}) async-start(bf16[8,2,18432]{2,1,0:T(2,128)(2,1)} %reshape.409), calls=%async_computation.1 | async-start | bytes 1179648 | tf_op jit(solution)/shard_map/all_to_all | solution.py:198
  329.1 13.1 %all-to-all-start.2 = ((bf16[8,16,768]{2,1,0:T(8,128)(2,1)}), bf16[8,16,768]{2,1,0:T(8,128)(2,1)S(1)}, u32[]{:S(2)}, u32[]{:S(2)}) async-start(bf16[8,16,768]{2,1,0:T(8,128)(2,1)} %reshape.356), calls=%async_computation.2 | async-start | bytes 393216 | tf_op jit(solution)/shard_map/all_to_all | solution.py:202
  332.5 13.5 %copy-start.29 = (bf16[128,128]{0,1:T(8,128)(2,1)S(1)}, bf16[128,128]{0,1:T(8,128)(2,1)}, u32[]{:S(2)}) copy-start(bf16[128,128]{0,1:T(8,128)(2,1)} %copy-done.28) | copy-start | bytes 98308
  342.2 18.6 %all-to-all-start.4 = ((bf16[8,16,2304]{2,1,0:T(8,128)(2,1)}), bf16[8,16,2304]{2,1,0:T(8,128)(2,1)S(1)}, u32[]{:S(2)}, u32[]{:S(2)}) async-start(bf16[8,16,2304]{2,1,0:T(8,128)(2,1)} %pad_maximum_fusion.2), calls=%async_computation.4 | async-start | bytes 1179648 | tf_op jit(solution)/shard_map/all_to_all | solution.py:202
  360.8 3.4 copy-start.37
  366.5 2.8 copy-start.53
  368.2 3.3 copy-start.10
  368.2 3.3 copy-start.23
  369.2 2.5 copy-start.32
  369.3 3.5 copy-start.51
  371.7 2.6 copy-start.13
  371.7 2.6 copy-start.21
  372.9 2.8 copy-start.49
  374.6 3.2 copy-start.12
  374.6 3.2 copy-start.19
  375.7 3.5 copy-start.47
  378.1 2.7 copy-start.17
  384.3 27.0 %collective-permute-start.6 = (bf16[128,768]{0,1:T(8,128)(2,1)S(1)}, bf16[128,768]{0,1:T(8,128)(2,1)S(1)}, u32[]{:S(2)}, u32[]{:S(2)}) collective-permute-start(bf16[128,768]{0,1:T(8,128)(2,1)S(1)} %get-tuple-element.2), channel_id=1, source_target_pairs={{0,2},{2,4},{4,6},{6,8},{8,10},{10,12},{12,14},{14,16},{16,18},{18... | collective-permute-start | bytes 589832 | tf_op jit(solution)/shard_map/ppermute | solution.py:20
  390.9 20.5 %collective-permute-start.7 = (bf16[128,768]{0,1:T(8,128)(2,1)S(1)}, bf16[128,768]{0,1:T(8,128)(2,1)S(1)}, u32[]{:S(2)}, u32[]{:S(2)}) collective-permute-start(bf16[128,768]{0,1:T(8,128)(2,1)S(1)} %get-tuple-element.3), channel_id=1, source_target_pairs={{2,0},{4,2},{6,4},{8,6},{10,8},{12,10},{14,12},{16,14},{18,16},{20... | collective-permute-start | bytes 589832 | tf_op jit(solution)/shard_map/ppermute | solution.py:22
  393.0 9.4 %copy-start.43 = (bf16[2,64,128]{2,1,0:T(8,128)(2,1)S(1)}, bf16[2,64,128]{2,1,0:T(8,128)(2,1)}, u32[]{:S(2)}) copy-start(bf16[2,64,128]{2,1,0:T(8,128)(2,1)} %fusion.47) | copy-start | bytes 98308
  393.0 9.4 %copy-start.42 = (bf16[2,64,128]{2,1,0:T(8,128)(2,1)S(1)}, bf16[2,64,128]{2,1,0:T(8,128)(2,1)}, u32[]{:S(2)}) copy-start(bf16[2,64,128]{2,1,0:T(8,128)(2,1)} %fusion.48) | copy-start | bytes 98308
  393.0 9.4 %copy-start.41 = (bf16[2,64,128]{2,1,0:T(8,128)(2,1)S(1)}, bf16[2,64,128]{2,1,0:T(8,128)(2,1)}, u32[]{:S(2)}) copy-start(bf16[2,64,128]{2,1,0:T(8,128)(2,1)} %fusion.49) | copy-start | bytes 98308
  393.0 9.4 %copy-start.40 = (bf16[2,64,128]{2,1,0:T(8,128)(2,1)S(1)}, bf16[2,64,128]{2,1,0:T(8,128)(2,1)}, u32[]{:S(2)}) copy-start(bf16[2,64,128]{2,1,0:T(8,128)(2,1)} %fusion.50) | copy-start | bytes 98308
  393.2 10.4 %collective-permute-start.4 = (bf16[128,768]{0,1:T(8,128)(2,1)S(1)}, bf16[128,768]{0,1:T(8,128)(2,1)S(1)}, u32[]{:S(2)}, u32[]{:S(2)}) collective-permute-start(bf16[128,768]{0,1:T(8,128)(2,1)S(1)} %get-tuple-element.4), channel_id=1, source_target_pairs={{0,2},{2,4},{4,6},{6,8},{8,10},{10,12},{12,14},{14,16},{16,18},{18... | collective-permute-start | bytes 589832 | tf_op jit(solution)/shard_map/ppermute | solution.py:20
  400.4 10.9 %collective-permute-start.5 = (bf16[128,768]{0,1:T(8,128)(2,1)S(1)}, bf16[128,768]{0,1:T(8,128)(2,1)S(1)}, u32[]{:S(2)}, u32[]{:S(2)}) collective-permute-start(bf16[128,768]{0,1:T(8,128)(2,1)S(1)} %get-tuple-element.5), channel_id=1, source_target_pairs={{2,0},{4,2},{6,4},{8,6},{10,8},{12,10},{14,12},{16,14},{18,16},{20... | collective-permute-start | bytes 589832 | tf_op jit(solution)/shard_map/ppermute | solution.py:22
  411.5 3.4 copy-start.56
  411.5 3.4 copy-start.58
  (25 other events, 32.1 us)
